TPU v7x, 32 devices: a whole 2x2x4 slice. The times are simulated.
32 devices in a mesh: slab: 4 (over y, x), rad: 8 (over z, core).
Axes of the slice: x: 2, y: 2, z: 4, core: 2. Of those that a mesh axis runs over, the one named last changes fastest.
Arguments:
- q_state: float32 [3, 524288], P(None, ('slab', 'rad')), may hold values from -6.71 to 6.71, as said below
- increments: float32 [3, 524288], P(None, ('slab', 'rad')), may hold values from -6 to 6
- velocity_grad: float32 [5, 12288], P(None, 'slab'), may hold values from -40 to 40
- element: int32 [524288], P(('slab', 'rad')), may hold values from 0 to 3071
- migration: int32 [524288], P(('slab', 'rad')), may hold values from -1 to 1, as said below
- volume: float32 [12288], P(('slab', 'rad')), may hold values from 14.222222 to 128
- div_map: float32 [192, 192], replicated, may hold values from -0.4375 to 0.4375
- stiffness: float32 [256, 4, 192, 192], P(('slab', 'rad')), may hold values from -0.06 to 1.06
- pattern: int32 [256, 4], P(('slab', 'rad')), may hold values from 0 to 191, as said below
- preconditioner: float32 [256, 192, 192], P(('slab', 'rad')), may hold values from -0.03 to 1.03
Outputs:
- q_out: float32 [3, 524288], P(None, ('slab', 'rad'))
- arrivals: float32 [2, 3, 32768], P(None, None, ('slab', 'rad'))
- element_stress: float32 [4, 12288], P(None, ('slab', 'rad'))
- velocity: float32 [256, 192], P(('slab', 'rad'))
Inputs may be any that keep to these rules, and one draw needn't show every extreme that they name: `q_state`: every dumbbell's stretch r^2 + z^2 + t^2 is below 45. Of the dumbbells of one device at most 1024 have migration 1 and at most 1024 have migration -1; some device has exactly 1024 with 1 and some device exactly 1024 with -1. pattern[b, 0] = 64 + b % 64; pattern[b, 1] lies in 0 .. 63, pattern[b, 2] in 64 .. 127, pattern[b, 3] in 128 .. 191.
All inputs are finite; a program needn't handle non-finite values.
Results may differ from a plain program's by a relative error of at most 0.0003.
Values sent between devices are 32-bit elements; how exact they have to be, the bound alone decides.
No kernel may reach another device: no remote copies, remote signals or barrier semaphores. Data moves between devices by JAX's collectives and lax.ppermute only.
A program may use at most 64 MiB of HBM per device.

v0:
```python
import math
import jax
import jax.numpy as jnp
from jax import lax
from jax.sharding import PartitionSpec as P

BLOCK = 192
ITERS = 6
extensibility = 50.0
time_step = 0.01
noise_scale = 0.1
damping = 0.6
highest = lax.Precision.HIGHEST


def passed_along(array, axis, by):
    size = lax.axis_size(axis)
    pairs = [(i, i + by) for i in range(size) if 0 <= i + by < size]
    return lax.ppermute(array, axis, pairs)


def extended(cells, sides, width):
    for axis, dim in sides:
        count = lax.axis_size(axis)
        ends = count - 1
        head = lax.slice_in_dim(cells, 0, width, axis=dim)
        tail = lax.slice_in_dim(cells, cells.shape[dim] - width, cells.shape[dim], axis=dim)
        cells = jnp.concatenate(
            [
                lax.ppermute(tail, axis, [(i, (i + 1) % count) for i in range(ends)]),
                cells,
                lax.ppermute(head, axis, [((i + 1) % count, i) for i in range(ends)]),
            ],
            axis=dim,
        )
    return cells


def update_dumbbells(q_here, inc_here, grads):
    radial = q_here[0]
    axial = q_here[1]
    azimuth = q_here[2]
    stretch = radial * radial + axial * axial + azimuth * azimuth
    spring = 1.0 / (1.0 - stretch / extensibility)
    drift = jnp.stack(
        [
            grads[0] * radial + grads[1] * axial,
            grads[2] * radial + grads[3] * axial,
            grads[4] * azimuth,
        ]
    )
    q_next = q_here + time_step * (drift - 0.5 * spring * q_here) + noise_scale * inc_here
    terms = jnp.stack(
        [
            spring * radial * radial - 1.0,
            spring * axial * axial - 1.0,
            spring * radial * axial,
            spring * azimuth * azimuth - 1.0,
        ]
    )
    return (q_next, terms)


def block_size(count):
    return math.gcd(count, 2048)


def split_onehots(index, count):
    upper_part = index // 128
    lower_part = index % 128
    hot_upper = (upper_part[None, :] == jnp.arange(count // 128, dtype=jnp.int32)[:, None]).astype(
        jnp.float32
    )
    hot_lower = (lower_part[None, :] == jnp.arange(128, dtype=jnp.int32)[:, None]).astype(
        jnp.float32
    )
    return (hot_upper, hot_lower)


def lookup_columns(table, index):
    rows, count = table.shape
    groups = count // 128
    arranged = table.reshape(rows, groups, 128).transpose(0, 2, 1).reshape(rows * 128, groups)
    size = block_size(index.shape[0])

    def one_block(indices):
        hot_upper, hot_lower = split_onehots(indices, count)
        picked = jnp.dot(arranged, hot_upper, precision=highest).reshape(rows, 128, size)
        return jnp.sum(picked * hot_lower[None], 1)

    result = lax.map(one_block, index.reshape(-1, size))
    return result.transpose(1, 0, 2).reshape(rows, -1)


def spread_block(values, indices, count):
    rows, size = values.shape
    hot_upper, hot_lower = split_onehots(indices, count)
    spread = (values[:, None, :] * hot_lower[None]).reshape(rows * 128, size)
    return lax.dot_general(spread, hot_upper, (((1,), (1,)), ((), ())), precision=highest)


def unarrange(total, rows, count):
    return total.reshape(rows, 128, count // 128).transpose(0, 2, 1).reshape(rows, count)


def accumulate_columns(values, index, count):
    rows = values.shape[0]
    size = block_size(index.shape[0])

    def accumulate_step(total, items):
        block_values, block_index = items
        return (total + spread_block(block_values, block_index, count), None)

    start = jnp.zeros((rows * 128, count // 128), jnp.float32)
    blocks = (values.reshape(rows, -1, size).transpose(1, 0, 2), index.reshape(-1, size))
    total, unused = lax.scan(accumulate_step, start, blocks)
    return unarrange(total, rows, count)


def pack_both(payload, migration, capacity):
    rows = payload.shape[0]
    padded_cap = -(-capacity // 128) * 128
    size = block_size(migration.shape[0])
    positions = jnp.arange(size, dtype=jnp.int32)
    earlier = (positions[:, None] < positions[None, :]).astype(jnp.bfloat16)

    def pack_step(carry, items):
        offsets, totals = carry
        block_values, block_moves = items
        chosen = jnp.stack([block_moves == 1, block_moves == -1])
        ranks = jnp.dot(
            chosen.astype(jnp.bfloat16), earlier, preferred_element_type=jnp.float32
        ).astype(jnp.int32)
        slots = jnp.where(chosen, offsets[:, None] + ranks, 0)
        filled = []
        for direction in range(2):
            masked = jnp.where(chosen[direction][None], block_values, 0.0)
            filled.append(spread_block(masked, slots[direction], padded_cap))
        offsets = offsets + jnp.sum(chosen.astype(jnp.int32), 1)
        return ((offsets, totals + jnp.stack(filled)), None)

    start = (jnp.zeros((2,), jnp.int32), jnp.zeros((2, rows * 128, padded_cap // 128), jnp.float32))
    blocks = (payload.reshape(rows, -1, size).transpose(1, 0, 2), migration.reshape(-1, size))
    (offsets, totals), unused = lax.scan(pack_step, start, blocks)
    upward = unarrange(totals[0], rows, padded_cap)
    downward = unarrange(totals[1], rows, padded_cap)
    return (upward, downward)


def body(
    q_state,
    increments,
    velocity_grad,
    element,
    migration,
    volume,
    div_map,
    stiffness,
    pattern,
    preconditioner,
):
    capacity = migration.shape[0] // 16
    slab_elems = velocity_grad.shape[1]
    grads = lookup_columns(velocity_grad, element)
    q_next, terms = update_dumbbells(q_state, increments, grads)
    payload = jnp.concatenate([q_next, terms, element.astype(jnp.float32)[None]], 0)
    upward, downward = pack_both(payload, migration, capacity)
    from_lower = passed_along(upward, "slab", 1)
    from_upper = passed_along(downward, "slab", -1)
    staying = jnp.where(migration == 0, terms, 0.0)
    all_terms = jnp.concatenate([staying, from_lower[3:7], from_upper[3:7]], 1)
    all_index = jnp.concatenate(
        [element, from_lower[7].astype(jnp.int32), from_upper[7].astype(jnp.int32)], 0
    )
    partial_value = accumulate_columns(all_terms, all_index, slab_elems)
    sums = lax.psum_scatter(partial_value, "rad", scatter_dimension=1, tiled=True)
    element_stress = sums / volume
    arrivals = jnp.stack([from_lower[0:3], from_upper[0:3]])
    own_blocks = stiffness.shape[0]
    groups = (
        element_stress.reshape(4, own_blocks, BLOCK // 4)
        .transpose(1, 0, 2)
        .reshape(own_blocks, BLOCK)
    )
    force = jnp.dot(groups, div_map, precision=highest)

    def precondition(vector):
        return jnp.einsum("bij,bj->bi", preconditioner, vector, precision=highest)

    window_rows = 3 * own_blocks * lax.axis_size("rad")
    selector = (
        pattern.reshape(-1)[:, None] == jnp.arange(window_rows, dtype=jnp.int32)[None, :]
    ).astype(jnp.float32)
    velocity = damping * precondition(force)
    for sweep_index in range(1, ITERS):
        gathered = lax.all_gather(velocity, "rad", axis=0, tiled=True)
        window = extended(gathered, (("slab", 0),), gathered.shape[0])
        neighbours = jnp.dot(selector, window, precision=highest).reshape(own_blocks, -1, BLOCK)
        image = jnp.einsum("bnij,bnj->bi", stiffness, neighbours, precision=highest)
        velocity = velocity + damping * precondition(force - image)
    return (q_next, arrivals, element_stress, velocity)


def solution(mesh):
    placed = (
        P(None, ("slab", "rad")),
        P(None, ("slab", "rad")),
        P(None, "slab"),
        P(("slab", "rad")),
        P(("slab", "rad")),
        P(("slab", "rad")),
        P(),
        P(("slab", "rad"), None, None, None),
        P(("slab", "rad"), None),
        P(("slab", "rad"), None, None),
    )
    return jax.shard_map(
        body,
        mesh=mesh,
        in_specs=placed,
        out_specs=(
            P(None, ("slab", "rad")),
            P(None, None, ("slab", "rad")),
            P(None, ("slab", "rad")),
            P(("slab", "rad"), None),
        ),
        check_vma=False,
    )
```

profile of v0, /device:TPU:4, one launch (start us, length us, event | category | flops | bytes accessed | tf_op | source)
XLA Modules:
  0.0 413.1 jit_solution(11150976871779817177)
XLA Ops:
  11.6 26.4 %while.41 = (s32[]{:T(128)}, f32[8,5,2048]{2,1,0:T(8,128)S(1)}, s32[8,2048]{1,0:T(8,128)S(1)}, f32[640,24]{0,1:T(8,128)S(1)}, s32[]{:T(128)}) while((s32[]{:T(128)}, f32[8,5,2048]{2,1,0:T(8,128)S(1)}, s32[8,2048]{1,0:T(8,128)S(1)}, f32[640,24]{0,1:T(8,128)S(1)}, s32[]{:T(128)}) %tuple.140), condition=%wide.region_2.3_spmd, body=%wide.region_0.2_spmd.sunk | while | flops 380719104 | bytes 12882001 | solution.py:91
  39.7 92.5 %while.42 = (s32[]{:T(128)}, s32[2]{0:T(128)S(1)}, f32[2,1024,8]{1,2,0:T(8,128)S(1)}, s32[8,2048]{1,0:T(8,128)S(1)}, f32[8,8,2048]{2,1,0:T(8,128)S(1)}, /*index=5*/s32[]{:T(128)}, s32[]{:T(128)}) while((s32[]{:T(128)}, s32[2]{0:T(128)S(1)}, f32[2,1024,8]{1,2,0:T(8,128)S(1)}, s32[8,2048]{1,0:T(8,128)S(1)}, ...), condition=%wide.region_5.6_spmd.clone, body=%wide.region_3.5_spmd.clone.sunk | while | flops 433287168 | bytes 38502552 | solution.py:144
  42.6 3.9 convolution_bitcast_fusion.4
  54.1 3.9 convolution_bitcast_fusion.4
  65.6 3.9 convolution_bitcast_fusion.4
  77.1 3.9 convolution_bitcast_fusion.4
  142.7 62.6 %while.43 = (s32[]{:T(128)}, f32[512,24]{0,1:T(8,128)S(1)}, f32[9,4,2048]{2,0,1:T(8,128)S(1)}, s32[9,2048]{1,0:T(8,128)S(1)}, s32[]{:T(128)}, /*index=5*/s32[]{:T(128)}) while((s32[]{:T(128)}, f32[512,24]{0,1:T(8,128)S(1)}, f32[9,4,2048]{2,0,1:T(8,128)S(1)}, s32[9,2048]{1,0:T(8,128)S(1)}, s32[]{:T(128)}, ...), condition=%wide.region_7.8_spmd.clone, body=%wide.region_6.7_spmd.clone.sunk | while | flops 303677440 | bytes 10805343 | solution.py:116
  145.6 4.2 %convolution_add_fusion.2 = f32[512,24]{0,1:T(8,128)S(1)} fusion(f32[512,2048]{1,0:T(8,128)} %bitcast.207, s32[2048]{0:T(1024)S(1)} %bitcast.214, f32[512,24]{0,1:T(8,128)S(1)} %get-tuple-element.504, pred[]{:T(512)S(6)} %compare.47), kind=kOutput, calls=%fused_computation.14.clone.1 | convolution fusion | flops 302063616 | bytes 4300801 | tf_op jit(solution)/shard_map/while/body/eval_jaxpr/dot_general | solution.py:99
  152.6 4.2 %convolution_add_fusion.2 = f32[512,24]{0,1:T(8,128)S(1)} fusion(f32[512,2048]{1,0:T(8,128)} %bitcast.207, s32[2048]{0:T(1024)S(1)} %bitcast.214, f32[512,24]{0,1:T(8,128)S(1)} %get-tuple-element.504, pred[]{:T(512)S(6)} %compare.47), kind=kOutput, calls=%fused_computation.14.clone.1 | convolution fusion | flops 302063616 | bytes 4300801 | tf_op jit(solution)/shard_map/while/body/eval_jaxpr/dot_general | solution.py:99
  159.5 4.2 %convolution_add_fusion.2 = f32[512,24]{0,1:T(8,128)S(1)} fusion(f32[512,2048]{1,0:T(8,128)} %bitcast.207, s32[2048]{0:T(1024)S(1)} %bitcast.214, f32[512,24]{0,1:T(8,128)S(1)} %get-tuple-element.504, pred[]{:T(512)S(6)} %compare.47), kind=kOutput, calls=%fused_computation.14.clone.1 | convolution fusion | flops 302063616 | bytes 4300801 | tf_op jit(solution)/shard_map/while/body/eval_jaxpr/dot_general | solution.py:99
  166.4 4.2 %convolution_add_fusion.2 = f32[512,24]{0,1:T(8,128)S(1)} fusion(f32[512,2048]{1,0:T(8,128)} %bitcast.207, s32[2048]{0:T(1024)S(1)} %bitcast.214, f32[512,24]{0,1:T(8,128)S(1)} %get-tuple-element.504, pred[]{:T(512)S(6)} %compare.47), kind=kOutput, calls=%fused_computation.14.clone.1 | convolution fusion | flops 302063616 | bytes 4300801 | tf_op jit(solution)/shard_map/while/body/eval_jaxpr/dot_general | solution.py:99
  173.4 4.2 %convolution_add_fusion.2 = f32[512,24]{0,1:T(8,128)S(1)} fusion(f32[512,2048]{1,0:T(8,128)} %bitcast.207, s32[2048]{0:T(1024)S(1)} %bitcast.214, f32[512,24]{0,1:T(8,128)S(1)} %get-tuple-element.504, pred[]{:T(512)S(6)} %compare.47), kind=kOutput, calls=%fused_computation.14.clone.1 | convolution fusion | flops 302063616 | bytes 4300801 | tf_op jit(solution)/shard_map/while/body/eval_jaxpr/dot_general | solution.py:99
  180.3 4.2 %convolution_add_fusion.2 = f32[512,24]{0,1:T(8,128)S(1)} fusion(f32[512,2048]{1,0:T(8,128)} %bitcast.207, s32[2048]{0:T(1024)S(1)} %bitcast.214, f32[512,24]{0,1:T(8,128)S(1)} %get-tuple-element.504, pred[]{:T(512)S(6)} %compare.47), kind=kOutput, calls=%fused_computation.14.clone.1 | convolution fusion | flops 302063616 | bytes 4300801 | tf_op jit(solution)/shard_map/while/body/eval_jaxpr/dot_general | solution.py:99
  187.3 4.2 %convolution_add_fusion.2 = f32[512,24]{0,1:T(8,128)S(1)} fusion(f32[512,2048]{1,0:T(8,128)} %bitcast.207, s32[2048]{0:T(1024)S(1)} %bitcast.214, f32[512,24]{0,1:T(8,128)S(1)} %get-tuple-element.504, pred[]{:T(512)S(6)} %compare.47), kind=kOutput, calls=%fused_computation.14.clone.1 | convolution fusion | flops 302063616 | bytes 4300801 | tf_op jit(solution)/shard_map/while/body/eval_jaxpr/dot_general | solution.py:99
  194.2 4.2 %convolution_add_fusion.2 = f32[512,24]{0,1:T(8,128)S(1)} fusion(f32[512,2048]{1,0:T(8,128)} %bitcast.207, s32[2048]{0:T(1024)S(1)} %bitcast.214, f32[512,24]{0,1:T(8,128)S(1)} %get-tuple-element.504, pred[]{:T(512)S(6)} %compare.47), kind=kOutput, calls=%fused_computation.14.clone.1 | convolution fusion | flops 302063616 | bytes 4300801 | tf_op jit(solution)/shard_map/while/body/eval_jaxpr/dot_general | solution.py:99
  201.1 4.2 %convolution_add_fusion.2 = f32[512,24]{0,1:T(8,128)S(1)} fusion(f32[512,2048]{1,0:T(8,128)} %bitcast.207, s32[2048]{0:T(1024)S(1)} %bitcast.214, f32[512,24]{0,1:T(8,128)S(1)} %get-tuple-element.504, pred[]{:T(512)S(6)} %compare.47), kind=kOutput, calls=%fused_computation.14.clone.1 | convolution fusion | flops 302063616 | bytes 4300801 | tf_op jit(solution)/shard_map/while/body/eval_jaxpr/dot_general | solution.py:99
  207.1 34.3 %reduce-scatter.4.cloned.1.call-done = f32[384,4]{1,0:T(8,128)} async-done(((f32[3072,4]{1,0:T(8,128)}), f32[384,4]{1,0:T(8,128)}) %reduce-scatter.4.cloned.1.call-update) | async-done | bytes 6160
  244.2 14.0 %all_gather.15 = f32[64,192]{1,0:T(8,128)S(1)} all-gather(f32[8,192]{1,0:T(8,128)S(1)} %bitcast_multiply_fusion.5), channel_id=1, replica_groups=mesh['slab'=4,'rad'=8] {'rad'}, dimensions={0}, use_global_device_ids=true | all-gather | bytes 55296 | tf_op jit(solution)/shard_map/all_gather | solution.py:196
  264.4 4.5 %collective-permute-done.2 = f32[64,192]{1,0:T(8,128)S(1)} collective-permute-done((f32[64,192]{1,0:T(8,128)S(1)}, f32[64,192]{1,0:T(8,128)S(1)}, u32[]{:S(2)}, u32[]{:S(2)}) %collective-permute-start.2) | collective-permute-done | bytes 49184 | tf_op jit(solution)/shard_map/ppermute | solution.py:30
  269.1 7.2 %fusion.95 = f32[8,1,192,1]{2,1,3,0:T(1,128)S(1)} fusion(f32[8,4,192,1]{2,3,1,0:T(1,128)S(1)} %reshape.325, f32[8,4,192,192]{3,2,1,0:T(8,128)} %param.23), kind=kOutput, calls=%fused_computation.172 | convolution fusion | flops 14155776 | bytes 4749312 | tf_op jit(solution)/shard_map/bnij,bnj->bi/dot_general | solution.py:199
  277.7 14.0 %all_gather.16 = f32[64,192]{1,0:T(8,128)S(1)} all-gather(f32[8,192]{1,0:T(8,128)S(1)} %fusion.71), channel_id=1, replica_groups=mesh['slab'=4,'rad'=8] {'rad'}, dimensions={0}, use_global_device_ids=true | all-gather | bytes 55296 | tf_op jit(solution)/shard_map/all_gather | solution.py:196
  293.6 3.9 collective-permute-start.4
  301.0 7.2 %fusion.96 = f32[8,1,192,1]{2,1,3,0:T(1,128)S(1)} fusion(f32[8,4,192,1]{2,3,1,0:T(1,128)S(1)} %reshape.327, f32[8,4,192,192]{3,2,1,0:T(8,128)} %param.23), kind=kOutput, calls=%fused_computation.173 | convolution fusion | flops 14155776 | bytes 4749312 | tf_op jit(solution)/shard_map/bnij,bnj->bi/dot_general | solution.py:199
  309.6 14.2 %all_gather.17 = f32[64,192]{1,0:T(8,128)S(1)} all-gather(f32[8,192]{1,0:T(8,128)S(1)} %fusion.69), channel_id=1, replica_groups=mesh['slab'=4,'rad'=8] {'rad'}, dimensions={0}, use_global_device_ids=true | all-gather | bytes 55296 | tf_op jit(solution)/shard_map/all_gather | solution.py:196
  325.7 3.9 collective-permute-start.6
  333.1 7.2 %fusion.97 = f32[8,1,192,1]{2,1,3,0:T(1,128)S(1)} fusion(f32[8,4,192,1]{2,3,1,0:T(1,128)S(1)} %reshape.329, f32[8,4,192,192]{3,2,1,0:T(8,128)} %param.23), kind=kOutput, calls=%fused_computation.174 | convolution fusion | flops 14155776 | bytes 4749312 | tf_op jit(solution)/shard_map/bnij,bnj->bi/dot_general | solution.py:199
  341.7 14.0 %all_gather.18 = f32[64,192]{1,0:T(8,128)S(1)} all-gather(f32[8,192]{1,0:T(8,128)S(1)} %fusion.67), channel_id=1, replica_groups=mesh['slab'=4,'rad'=8] {'rad'}, dimensions={0}, use_global_device_ids=true | all-gather | bytes 55296 | tf_op jit(solution)/shard_map/all_gather | solution.py:196
  357.6 3.9 collective-permute-start.8
  365.0 7.2 %fusion.98 = f32[8,1,192,1]{2,1,3,0:T(1,128)S(1)} fusion(f32[8,4,192,1]{2,3,1,0:T(1,128)S(1)} %reshape.331, f32[8,4,192,192]{3,2,1,0:T(8,128)} %param.23), kind=kOutput, calls=%fused_computation.175 | convolution fusion | flops 14155776 | bytes 4749312 | tf_op jit(solution)/shard_map/bnij,bnj->bi/dot_general | solution.py:199
  373.5 14.0 %all_gather.19 = f32[64,192]{1,0:T(8,128)S(1)} all-gather(f32[8,192]{1,0:T(8,128)S(1)} %fusion.65), channel_id=1, replica_groups=mesh['slab'=4,'rad'=8] {'rad'}, dimensions={0}, use_global_device_ids=true | all-gather | bytes 55296 | tf_op jit(solution)/shard_map/all_gather | solution.py:196
  389.5 3.9 collective-permute-start.10
  396.8 7.2 %fusion.99 = f32[8,1,192,1]{2,1,3,0:T(1,128)S(1)} fusion(f32[8,4,192,1]{2,3,1,0:T(1,128)S(1)} %reshape.333, f32[8,4,192,192]{3,2,1,0:T(8,128)} %param.23), kind=kOutput, calls=%fused_computation.176 | convolution fusion | flops 14155776 | bytes 4749312 | tf_op jit(solution)/shard_map/bnij,bnj->bi/dot_general | solution.py:199
  (318 shorter events, 182.0 us)
Async XLA Ops:
  7.2 235.6 %copy-start = (f32[8,192,192]{2,1,0:T(8,128)S(1)}, f32[8,192,192]{2,1,0:T(8,128)}, u32[]{:S(2)}) copy-start(f32[8,192,192]{2,1,0:T(8,128)} %param.25) | copy-start | bytes 3538948
  7.2 234.2 %reduce-scatter.4.cloned.1.call-start = ((), (), s32[]{:S(2)}) async-start(), calls=%async_computation.1 | async-start | bytes 1769472
  11.5 26.7 %copy-start.4 = (s32[16384]{0:T(1024)S(1)}, s32[16384]{0:T(1024)}, u32[]{:S(2)}) copy-start(s32[16384]{0:T(1024)} %param.20) | copy-start | bytes 196612
  11.5 26.7 %copy-start.1 = (f32[3,16384]{1,0:T(4,128)S(1)}, f32[3,16384]{1,0:T(4,128)}, u32[]{:S(2)}) copy-start(f32[3,16384]{1,0:T(4,128)} %param.16) | copy-start | bytes 589828
  11.5 27.1 %copy-start.5 = (f32[3,16384]{1,0:T(4,128)S(1)}, f32[3,16384]{1,0:T(4,128)}, u32[]{:S(2)}) copy-start(f32[3,16384]{1,0:T(4,128)} %param.17) | copy-start | bytes 589828
  39.0 0.7 copy-start.2
  39.7 103.0 %copy-start.3 = (s32[16384]{0:T(1024)S(1)}, s32[16384]{0:T(1024)}, u32[]{:S(2)}) copy-start(s32[16384]{0:T(1024)} %param.19) | copy-start | bytes 196612
  132.2 6.2 %collective-permute-start.1 = (f32[8,1024]{1,0:T(8,128)S(1)}, f32[8,1024]{1,0:T(8,128)S(1)}, u32[]{:S(2)}, u32[]{:S(2)}) collective-permute-start(f32[8,1024]{1,0:T(8,128)S(1)} %bitcast.238), channel_id=1, source_target_pairs={{8,0},{16,8},{24,16},{9,1},{17,9},{25,17},{10,2},{18,10},{26,18},{... | collective-permute-start | bytes 98312 | tf_op jit(solution)/shard_map/ppermute | solution.py:19
  135.6 6.7 %collective-permute-start = (f32[8,1024]{1,0:T(8,128)S(1)}, f32[8,1024]{1,0:T(8,128)S(1)}, u32[]{:S(2)}, u32[]{:S(2)}) collective-permute-start(f32[8,1024]{1,0:T(8,128)S(1)} %bitcast.239), channel_id=1, source_target_pairs={{0,8},{8,16},{16,24},{1,9},{9,17},{17,25},{2,10},{10,18},{18,26},{... | collective-permute-start | bytes 98312 | tf_op jit(solution)/shard_map/ppermute | solution.py:19
  142.7 99.7 %copy-start.8 = (f32[384]{0:T(512)S(1)}, f32[384]{0:T(512)}, u32[]{:S(2)}) copy-start(f32[384]{0:T(512)} %param.21) | copy-start | bytes 4612
  142.7 99.9 %copy-start.6 = (f32[192,192]{1,0:T(8,128)S(1)}, f32[192,192]{1,0:T(8,128)}, u32[]{:S(2)}) copy-start(f32[192,192]{1,0:T(8,128)} %param.22) | copy-start | bytes 442372
  142.7 121.3 %copy-start.9 = (s32[8,4]{0,1:T(4,128)S(1)}, s32[8,4]{0,1:T(4,128)}, u32[]{:S(2)}) copy-start(s32[8,4]{0,1:T(4,128)} %param.24) | copy-start | bytes 388
  242.5 65.7 %copy-start.7 = (f32[4,384]{1,0:T(4,128)}, f32[4,384]{1,0:T(4,128)S(1)}, u32[]{:S(2)}) copy-start(f32[4,384]{1,0:T(4,128)S(1)} %broadcast_divide_fusion) | copy-start | bytes 18436
  258.2 6.2 %collective-permute-start.3 = (f32[64,192]{1,0:T(8,128)S(1)}, f32[64,192]{1,0:T(8,128)S(1)}, u32[]{:S(2)}, u32[]{:S(2)}) collective-permute-start(f32[64,192]{1,0:T(8,128)S(1)} %all_gather.15), channel_id=1, source_target_pairs={{8,0},{16,8},{24,16},{9,1},{17,9},{25,17},{10,2},{18,10},{26,18},{... | collective-permute-start | bytes 147464 | tf_op jit(solution)/shard_map/ppermute | solution.py:32
  261.8 7.1 %collective-permute-start.2 = (f32[64,192]{1,0:T(8,128)S(1)}, f32[64,192]{1,0:T(8,128)S(1)}, u32[]{:S(2)}, u32[]{:S(2)}) collective-permute-start(f32[64,192]{1,0:T(8,128)S(1)} %all_gather.15), channel_id=1, source_target_pairs={{0,8},{8,16},{16,24},{1,9},{9,17},{17,25},{2,10},{10,18},{18,26},{... | collective-permute-start | bytes 147464 | tf_op jit(solution)/shard_map/ppermute | solution.py:30
  291.7 6.2 %collective-permute-start.5 = (f32[64,192]{1,0:T(8,128)S(1)}, f32[64,192]{1,0:T(8,128)S(1)}, u32[]{:S(2)}, u32[]{:S(2)}) collective-permute-start(f32[64,192]{1,0:T(8,128)S(1)} %all_gather.16), channel_id=1, source_target_pairs={{8,0},{16,8},{24,16},{9,1},{17,9},{25,17},{10,2},{18,10},{26,18},{... | collective-permute-start | bytes 147464 | tf_op jit(solution)/shard_map/ppermute | solution.py:32
  293.6 7.1 %collective-permute-start.4 = (f32[64,192]{1,0:T(8,128)S(1)}, f32[64,192]{1,0:T(8,128)S(1)}, u32[]{:S(2)}, u32[]{:S(2)}) collective-permute-start(f32[64,192]{1,0:T(8,128)S(1)} %all_gather.16), channel_id=1, source_target_pairs={{0,8},{8,16},{16,24},{1,9},{9,17},{17,25},{2,10},{10,18},{18,26},{... | collective-permute-start | bytes 147464 | tf_op jit(solution)/shard_map/ppermute | solution.py:30
  323.8 6.2 %collective-permute-start.7 = (f32[64,192]{1,0:T(8,128)S(1)}, f32[64,192]{1,0:T(8,128)S(1)}, u32[]{:S(2)}, u32[]{:S(2)}) collective-permute-start(f32[64,192]{1,0:T(8,128)S(1)} %all_gather.17), channel_id=1, source_target_pairs={{8,0},{16,8},{24,16},{9,1},{17,9},{25,17},{10,2},{18,10},{26,18},{... | collective-permute-start | bytes 147464 | tf_op jit(solution)/shard_map/ppermute | solution.py:32
  325.7 7.1 %collective-permute-start.6 = (f32[64,192]{1,0:T(8,128)S(1)}, f32[64,192]{1,0:T(8,128)S(1)}, u32[]{:S(2)}, u32[]{:S(2)}) collective-permute-start(f32[64,192]{1,0:T(8,128)S(1)} %all_gather.17), channel_id=1, source_target_pairs={{0,8},{8,16},{16,24},{1,9},{9,17},{17,25},{2,10},{10,18},{18,26},{... | collective-permute-start | bytes 147464 | tf_op jit(solution)/shard_map/ppermute | solution.py:30
  355.7 6.2 %collective-permute-start.9 = (f32[64,192]{1,0:T(8,128)S(1)}, f32[64,192]{1,0:T(8,128)S(1)}, u32[]{:S(2)}, u32[]{:S(2)}) collective-permute-start(f32[64,192]{1,0:T(8,128)S(1)} %all_gather.18), channel_id=1, source_target_pairs={{8,0},{16,8},{24,16},{9,1},{17,9},{25,17},{10,2},{18,10},{26,18},{... | collective-permute-start | bytes 147464 | tf_op jit(solution)/shard_map/ppermute | solution.py:32
  357.6 7.1 %collective-permute-start.8 = (f32[64,192]{1,0:T(8,128)S(1)}, f32[64,192]{1,0:T(8,128)S(1)}, u32[]{:S(2)}, u32[]{:S(2)}) collective-permute-start(f32[64,192]{1,0:T(8,128)S(1)} %all_gather.18), channel_id=1, source_target_pairs={{0,8},{8,16},{16,24},{1,9},{9,17},{17,25},{2,10},{10,18},{18,26},{... | collective-permute-start | bytes 147464 | tf_op jit(solution)/shard_map/ppermute | solution.py:30
  387.5 6.5 %collective-permute-start.11 = (f32[64,192]{1,0:T(8,128)S(1)}, f32[64,192]{1,0:T(8,128)S(1)}, u32[]{:S(2)}, u32[]{:S(2)}) collective-permute-start(f32[64,192]{1,0:T(8,128)S(1)} %all_gather.19), channel_id=1, source_target_pairs={{8,0},{16,8},{24,16},{9,1},{17,9},{25,17},{10,2},{18,10},{26,18},{... | collective-permute-start | bytes 147464 | tf_op jit(solution)/shard_map/ppermute | solution.py:32
  389.5 7.1 %collective-permute-start.10 = (f32[64,192]{1,0:T(8,128)S(1)}, f32[64,192]{1,0:T(8,128)S(1)}, u32[]{:S(2)}, u32[]{:S(2)}) collective-permute-start(f32[64,192]{1,0:T(8,128)S(1)} %all_gather.19), channel_id=1, source_target_pairs={{0,8},{8,16},{16,24},{1,9},{9,17},{17,25},{2,10},{10,18},{18,26},{... | collective-permute-start | bytes 147464 | tf_op jit(solution)/shard_map/ppermute | solution.py:30
Sparse Core Ops, SparseCore 0:
  207.2 34.1 reduce-scatter.3
where the time goes:
time: 418 us; the launch traced here: 413 us
  matrix products  170 us (41%)
  blocking collectives  70.2 us (17%)
  other arithmetic  58 us (14%)
  waiting for transfers between devices  54.9 us (13%)
  starting transfers between devices  35 us (8%)
  between operations  14.9 us (4%)
  local copies, waits for them, and re-layouts  7.52 us (2%)
    dot_general x25, matrix products, spread_block(): lax.dot_general(spread, hot_upper, (((1,), (1,)), ((), ())), precision=hi...  100 us
    all_gather x5, blocking collectives, body(): gathered = lax.all_gather(velocity, 'rad', axis=0, tiled=True)  70.2 us
    mul x25, other arithmetic, spread_block(): spread = (values[:, None, :] * hot_lower[None]).reshape(rows * 128, size)  39.8 us
    dot_general x5, matrix products, body(): image = jnp.einsum('bnij,bnj->bi', stiffness, neighbours, precision=highest)  35.9 us
    unnamed x2, waiting for transfers between devices  34.3 us
    dot_general x8, matrix products, one_block(): jnp.dot(arranged, hot_upper, precision=highest).reshape(rows, 128, size)  18.2 us
    ppermute x5, starting transfers between devices, extended(): lax.ppermute(tail, axis, [(i, (i + 1) % count) for i in range(ends)])  17.9 us
    ppermute x5, waiting for transfers between devices, extended(): lax.ppermute(tail, axis, [(i, (i + 1) % count) for i in range(ends)])  15.5 us
  transfers between devices with their start and end apart: 13, of which 11 were waited for; matrix products, arithmetic and copies ran while one was open for 0% of the time, Pallas kernels for 0%

commit v1 on v0

--- a/solution.py
+++ b/solution.py
@@ -193,7 +193,20 @@
     ).astype(jnp.float32)
     velocity = damping * precondition(force)
     for sweep_index in range(1, ITERS):
-        gathered = lax.all_gather(velocity, "rad", axis=0, tiled=True)
+
+        def begin_streams(view):
+            full_n = lax.axis_size("rad")
+            odd = [None] * full_n
+            odd[full_n - 1] = view
+            parts_seen = [(i0, (i0 + 1) % full_n) for i0 in range(full_n)]
+            for no in range(full_n - 2, -1, -1):
+                odd[no] = lax.ppermute(odd[no + 1], "rad", parts_seen)
+            base_arr = jnp.concatenate(odd, 0)
+            a_now = (lax.axis_index("rad") + 1) * view.shape[0]
+            small = jnp.roll(base_arr, a_now, axis=0)
+            return small
+
+        gathered = begin_streams(velocity)
         window = extended(gathered, (("slab", 0),), gathered.shape[0])
         neighbours = jnp.dot(selector, window, precision=highest).reshape(own_blocks, -1, BLOCK)
         image = jnp.einsum("bnij,bnj->bi", stiffness, neighbours, precision=highest)

time: 418 us -> 520 us (1.24)
  waiting for transfers between devices: 54.9 us -> 225 us
  blocking collectives: 70.2 us -> 0 us
    ppermute x0 -> x35, waiting for transfers between devices: none -> 171 us  [begin_streams(): odd[no] = lax.ppermute(odd[no + 1], 'rad', parts_seen)]
    all_gather x5 -> x0, blocking collectives: 70.2 us -> none  [body(): gathered = lax.all_gather(velocity, 'rad', axis=0, tiled=True)]
  transfers between devices with their start and end apart: 13 -> 48, of which waited for: 11 -> 46; matrix products, arithmetic and copies ran while one was open for 0% -> 0% of each run, Pallas kernels for 0% -> 0%
where the time goes in v1:
time: 520 us; the launch traced here: 515 us
  waiting for transfers between devices  225 us (43%)
  matrix products  171 us (33%)
  other arithmetic  58.7 us (11%)
  starting transfers between devices  35.5 us (7%)
  between operations  15.2 us (3%)
  local copies, waits for them, and re-layouts  7.62 us (1%)
    ppermute x35, waiting for transfers between devices, begin_streams(): odd[no] = lax.ppermute(odd[no + 1], 'rad', parts_seen)  171 us
    dot_general x25, matrix products, spread_block(): lax.dot_general(spread, hot_upper, (((1,), (1,)), ((), ())), precision=hi...  100 us
    mul x25, other arithmetic, spread_block(): spread = (values[:, None, :] * hot_lower[None]).reshape(rows * 128, size)  40.3 us
    dot_general x5, matrix products, body(): image = jnp.einsum('bnij,bnj->bi', stiffness, neighbours, precision=highest)  36.2 us
    unnamed x2, waiting for transfers between devices  34.6 us
    ppermute x5, starting transfers between devices, extended(): lax.ppermute(tail, axis, [(i, (i + 1) % count) for i in range(ends)])  18.4 us
    dot_general x8, matrix products, one_block(): jnp.dot(arranged, hot_upper, precision=highest).reshape(rows, 128, size)  18.2 us
    ppermute x5, waiting for transfers between devices, extended(): lax.ppermute(tail, axis, [(i, (i + 1) % count) for i in range(ends)])  15 us
  transfers between devices with their start and end apart: 48, of which 46 were waited for; matrix products, arithmetic and copies ran while one was open for 0% of the time, Pallas kernels for 0%

profile of v1, /device:TPU:4, one launch (start us, length us, event | category | flops | bytes accessed | tf_op | source)
XLA Modules:
  0.0 514.9 jit_solution(7177508204410388123)
XLA Ops:
  11.6 26.4 %while.41 = (s32[]{:T(128)}, f32[8,5,2048]{2,1,0:T(8,128)S(1)}, s32[8,2048]{1,0:T(8,128)S(1)}, f32[640,24]{0,1:T(8,128)S(1)}, s32[]{:T(128)}) while((s32[]{:T(128)}, f32[8,5,2048]{2,1,0:T(8,128)S(1)}, s32[8,2048]{1,0:T(8,128)S(1)}, f32[640,24]{0,1:T(8,128)S(1)}, s32[]{:T(128)}) %tuple.141), condition=%wide.region_2.3_spmd, body=%wide.region_0.2_spmd.sunk | while | flops 380719104 | bytes 12882001 | solution.py:91
  39.7 92.6 %while.42 = (s32[]{:T(128)}, s32[2]{0:T(128)S(1)}, f32[2,1024,8]{1,2,0:T(8,128)S(1)}, s32[8,2048]{1,0:T(8,128)S(1)}, f32[8,8,2048]{2,1,0:T(8,128)S(1)}, /*index=5*/s32[]{:T(128)}, s32[]{:T(128)}) while((s32[]{:T(128)}, s32[2]{0:T(128)S(1)}, f32[2,1024,8]{1,2,0:T(8,128)S(1)}, s32[8,2048]{1,0:T(8,128)S(1)}, ...), condition=%wide.region_5.6_spmd.clone, body=%wide.region_3.5_spmd.clone.sunk | while | flops 433287168 | bytes 38502552 | solution.py:144
  142.8 63.1 %while.43 = (s32[]{:T(128)}, f32[512,24]{0,1:T(8,128)S(1)}, f32[9,4,2048]{2,0,1:T(8,128)S(1)}, s32[9,2048]{1,0:T(8,128)S(1)}, s32[]{:T(128)}, /*index=5*/s32[]{:T(128)}) while((s32[]{:T(128)}, f32[512,24]{0,1:T(8,128)S(1)}, f32[9,4,2048]{2,0,1:T(8,128)S(1)}, s32[9,2048]{1,0:T(8,128)S(1)}, s32[]{:T(128)}, ...), condition=%wide.region_7.8_spmd.clone, body=%wide.region_6.7_spmd.clone.sunk | while | flops 303677440 | bytes 10805343 | solution.py:116
  207.6 34.6 %reduce-scatter.4.cloned.1.call-done = f32[384,4]{1,0:T(8,128)} async-done(((f32[3072,4]{1,0:T(8,128)}), f32[384,4]{1,0:T(8,128)}) %reduce-scatter.4.cloned.1.call-update) | async-done | bytes 6160
  245.1 4.9 collective-permute-done.2
  250.0 4.9 collective-permute-done.3
  264.6 4.9 collective-permute-done.6
  269.5 4.9 collective-permute-done.7
  274.3 4.9 collective-permute-done.8
  289.8 7.2 %fusion.100 = f32[8,1,192,1]{2,1,3,0:T(1,128)S(1)} fusion(f32[8,4,192,1]{2,3,1,0:T(1,128)S(1)} %reshape.325, f32[8,4,192,192]{3,2,1,0:T(8,128)} %param.25), kind=kOutput, calls=%fused_computation.227 | convolution fusion | flops 14155776 | bytes 4749312 | tf_op jit(solution)/shard_map/bnij,bnj->bi/dot_general | solution.py:212
  298.4 4.9 collective-permute-done.11
  313.0 4.9 collective-permute-done.14
  317.9 4.9 collective-permute-done.15
  322.8 4.9 collective-permute-done.16
  327.6 4.9 collective-permute-done.17
  341.9 7.4 %fusion.101 = f32[8,1,192,1]{2,1,3,0:T(1,128)S(1)} fusion(f32[8,4,192,1]{2,3,1,0:T(1,128)S(1)} %reshape.327, f32[8,4,192,192]{3,2,1,0:T(8,128)} %param.25), kind=kOutput, calls=%fused_computation.228 | convolution fusion | flops 14155776 | bytes 4749312 | tf_op jit(solution)/shard_map/bnij,bnj->bi/dot_general | solution.py:212
  350.7 4.9 collective-permute-done.20
  355.6 4.9 collective-permute-done.21
  375.1 4.9 collective-permute-done.25
  380.0 4.9 collective-permute-done.26
  394.2 7.2 %fusion.102 = f32[8,1,192,1]{2,1,3,0:T(1,128)S(1)} fusion(f32[8,4,192,1]{2,3,1,0:T(1,128)S(1)} %reshape.329, f32[8,4,192,192]{3,2,1,0:T(8,128)} %param.25), kind=kOutput, calls=%fused_computation.229 | convolution fusion | flops 14155776 | bytes 4749312 | tf_op jit(solution)/shard_map/bnij,bnj->bi/dot_general | solution.py:212
  402.8 4.9 collective-permute-done.29
  407.7 4.9 collective-permute-done.30
  412.6 4.9 collective-permute-done.31
  427.2 4.9 collective-permute-done.34
  432.1 4.9 collective-permute-done.35
  446.3 7.2 %fusion.103 = f32[8,1,192,1]{2,1,3,0:T(1,128)S(1)} fusion(f32[8,4,192,1]{2,3,1,0:T(1,128)S(1)} %reshape.331, f32[8,4,192,192]{3,2,1,0:T(8,128)} %param.25), kind=kOutput, calls=%fused_computation.230 | convolution fusion | flops 14155776 | bytes 4749312 | tf_op jit(solution)/shard_map/bnij,bnj->bi/dot_general | solution.py:212
  454.9 4.9 collective-permute-done.38
  459.8 4.9 collective-permute-done.39
  464.6 4.9 collective-permute-done.40
  469.5 4.9 collective-permute-done.41
  498.6 7.2 %fusion.104 = f32[8,1,192,1]{2,1,3,0:T(1,128)S(1)} fusion(f32[8,4,192,1]{2,3,1,0:T(1,128)S(1)} %reshape.333, f32[8,4,192,192]{3,2,1,0:T(8,128)} %param.25), kind=kOutput, calls=%fused_computation.231 | convolution fusion | flops 14155776 | bytes 4749312 | tf_op jit(solution)/shard_map/bnij,bnj->bi/dot_general | solution.py:212
  (428 shorter events, 314.5 us)
Async XLA Ops:
  7.2 235.1 %reduce-scatter.4.cloned.1.call-start = ((), (), s32[]{:S(2)}) async-start(), calls=%async_computation.1 | async-start | bytes 1769472
  132.3 6.2 %collective-permute-start.1 = (f32[8,1024]{1,0:T(8,128)S(1)}, f32[8,1024]{1,0:T(8,128)S(1)}, u32[]{:S(2)}, u32[]{:S(2)}) collective-permute-start(f32[8,1024]{1,0:T(8,128)S(1)} %bitcast.240), channel_id=1, source_target_pairs={{8,0},{16,8},{24,16},{9,1},{17,9},{25,17},{10,2},{18,10},{26,18},{... | collective-permute-start | bytes 98312 | tf_op jit(solution)/shard_map/ppermute | solution.py:19
  135.7 6.7 %collective-permute-start = (f32[8,1024]{1,0:T(8,128)S(1)}, f32[8,1024]{1,0:T(8,128)S(1)}, u32[]{:S(2)}, u32[]{:S(2)}) collective-permute-start(f32[8,1024]{1,0:T(8,128)S(1)} %bitcast.241), channel_id=1, source_target_pairs={{0,8},{8,16},{16,24},{1,9},{9,17},{17,25},{2,10},{10,18},{18,26},{... | collective-permute-start | bytes 98312 | tf_op jit(solution)/shard_map/ppermute | solution.py:19
  245.1 4.9 collective-permute-start.2
  250.0 4.9 collective-permute-start.3
  269.5 4.9 collective-permute-start.7
  274.3 4.9 collective-permute-start.8
  279.3 6.2 %collective-permute-start.10 = (f32[64,192]{1,0:T(8,128)S(1)}, f32[64,192]{1,0:T(8,128)S(1)}, u32[]{:S(2)}, u32[]{:S(2)}) collective-permute-start(f32[64,192]{1,0:T(8,128)S(1)} %fusion.62), channel_id=1, source_target_pairs={{8,0},{16,8},{24,16},{9,1},{17,9},{25,17},{10,2},{18,10},{26,18},{... | collective-permute-start | bytes 147464 | tf_op jit(solution)/shard_map/ppermute | solution.py:32
  282.4 7.1 %collective-permute-start.9 = (f32[64,192]{1,0:T(8,128)S(1)}, f32[64,192]{1,0:T(8,128)S(1)}, u32[]{:S(2)}, u32[]{:S(2)}) collective-permute-start(f32[64,192]{1,0:T(8,128)S(1)} %fusion.62), channel_id=1, source_target_pairs={{0,8},{8,16},{16,24},{1,9},{9,17},{17,25},{2,10},{10,18},{18,26},{... | collective-permute-start | bytes 147464 | tf_op jit(solution)/shard_map/ppermute | solution.py:30
  298.4 4.9 collective-permute-start.11
  317.9 4.9 collective-permute-start.15
  322.8 4.9 collective-permute-start.16
  327.6 4.9 collective-permute-start.17
  332.6 6.2 %collective-permute-start.19 = (f32[64,192]{1,0:T(8,128)S(1)}, f32[64,192]{1,0:T(8,128)S(1)}, u32[]{:S(2)}, u32[]{:S(2)}) collective-permute-start(f32[64,192]{1,0:T(8,128)S(1)} %fusion.61), channel_id=1, source_target_pairs={{8,0},{16,8},{24,16},{9,1},{17,9},{25,17},{10,2},{18,10},{26,18},{... | collective-permute-start | bytes 147464 | tf_op jit(solution)/shard_map/ppermute | solution.py:32
  334.6 7.1 %collective-permute-start.18 = (f32[64,192]{1,0:T(8,128)S(1)}, f32[64,192]{1,0:T(8,128)S(1)}, u32[]{:S(2)}, u32[]{:S(2)}) collective-permute-start(f32[64,192]{1,0:T(8,128)S(1)} %fusion.61), channel_id=1, source_target_pairs={{0,8},{8,16},{16,24},{1,9},{9,17},{17,25},{2,10},{10,18},{18,26},{... | collective-permute-start | bytes 147464 | tf_op jit(solution)/shard_map/ppermute | solution.py:30
  350.7 4.9 collective-permute-start.20
  355.6 4.9 collective-permute-start.21
  375.1 4.9 collective-permute-start.25
  380.0 4.9 collective-permute-start.26
  384.9 6.2 %collective-permute-start.28 = (f32[64,192]{1,0:T(8,128)S(1)}, f32[64,192]{1,0:T(8,128)S(1)}, u32[]{:S(2)}, u32[]{:S(2)}) collective-permute-start(f32[64,192]{1,0:T(8,128)S(1)} %fusion.60), channel_id=1, source_target_pairs={{8,0},{16,8},{24,16},{9,1},{17,9},{25,17},{10,2},{18,10},{26,18},{... | collective-permute-start | bytes 147464 | tf_op jit(solution)/shard_map/ppermute | solution.py:32
  386.9 7.1 %collective-permute-start.27 = (f32[64,192]{1,0:T(8,128)S(1)}, f32[64,192]{1,0:T(8,128)S(1)}, u32[]{:S(2)}, u32[]{:S(2)}) collective-permute-start(f32[64,192]{1,0:T(8,128)S(1)} %fusion.60), channel_id=1, source_target_pairs={{0,8},{8,16},{16,24},{1,9},{9,17},{17,25},{2,10},{10,18},{18,26},{... | collective-permute-start | bytes 147464 | tf_op jit(solution)/shard_map/ppermute | solution.py:30
  402.8 4.9 collective-permute-start.29
  407.7 4.9 collective-permute-start.30
  412.6 4.9 collective-permute-start.31
  432.1 4.9 collective-permute-start.35
  437.0 6.2 %collective-permute-start.37 = (f32[64,192]{1,0:T(8,128)S(1)}, f32[64,192]{1,0:T(8,128)S(1)}, u32[]{:S(2)}, u32[]{:S(2)}) collective-permute-start(f32[64,192]{1,0:T(8,128)S(1)} %fusion.59), channel_id=1, source_target_pairs={{8,0},{16,8},{24,16},{9,1},{17,9},{25,17},{10,2},{18,10},{26,18},{... | collective-permute-start | bytes 147464 | tf_op jit(solution)/shard_map/ppermute | solution.py:32
  439.0 7.1 %collective-permute-start.36 = (f32[64,192]{1,0:T(8,128)S(1)}, f32[64,192]{1,0:T(8,128)S(1)}, u32[]{:S(2)}, u32[]{:S(2)}) collective-permute-start(f32[64,192]{1,0:T(8,128)S(1)} %fusion.59), channel_id=1, source_target_pairs={{0,8},{8,16},{16,24},{1,9},{9,17},{17,25},{2,10},{10,18},{18,26},{... | collective-permute-start | bytes 147464 | tf_op jit(solution)/shard_map/ppermute | solution.py:30
  454.9 4.9 collective-permute-start.38
  464.6 4.9 collective-permute-start.40
  484.1 5.1 collective-permute-start.44
  489.3 6.5 %collective-permute-start.46 = (f32[64,192]{1,0:T(8,128)S(1)}, f32[64,192]{1,0:T(8,128)S(1)}, u32[]{:S(2)}, u32[]{:S(2)}) collective-permute-start(f32[64,192]{1,0:T(8,128)S(1)} %fusion.58), channel_id=1, source_target_pairs={{8,0},{16,8},{24,16},{9,1},{17,9},{25,17},{10,2},{18,10},{26,18},{... | collective-permute-start | bytes 147464 | tf_op jit(solution)/shard_map/ppermute | solution.py:32
  491.3 7.1 %collective-permute-start.45 = (f32[64,192]{1,0:T(8,128)S(1)}, f32[64,192]{1,0:T(8,128)S(1)}, u32[]{:S(2)}, u32[]{:S(2)}) collective-permute-start(f32[64,192]{1,0:T(8,128)S(1)} %fusion.58), channel_id=1, source_target_pairs={{0,8},{8,16},{16,24},{1,9},{9,17},{17,25},{2,10},{10,18},{18,26},{... | collective-permute-start | bytes 147464 | tf_op jit(solution)/shard_map/ppermute | solution.py:30
  (26 other events, 948.4 us)
Sparse Core Ops, SparseCore 0:
  207.8 34.4 reduce-scatter.3
